TPU v7x, 32 devices: a whole 2x2x4 slice. The times are simulated.
32 devices in a mesh: blk: 4 (over y, x), group: 8 (over z, core).
Axes of the slice: x: 2, y: 2, z: 4, core: 2. Of those that a mesh axis runs over, the one named last changes fastest.
Arguments:
- picture_vector_list: bfloat16 [8, 1024, 768], P('group', 'blk'), may hold values from -0.25 to 0.25
- caption_latent_matrix: bfloat16 [8, 1024, 3072], P('group', 'blk'), may hold values from -6 to 6
- linear_map_matrix: bfloat16 [3072, 768], P('group'), may hold values from -0.109375 to 0.109375
- target_match_index: int32 [8, 1024], P('group', 'blk'), may hold values from 0 to 1023, each once within a row
- sharpness_factor: float32 [1], replicated, may hold values from 24 to 40
- offset_term: float32 [1], replicated, may hold values from -6 to -5
Outputs:
- row_loss: float32 [8, 1024], P('group', 'blk')
- image_grad: bfloat16 [8, 1024, 768], P('group', 'blk')
- projection_grad: float32 [3072, 768], P(('blk', 'group'))
Inputs may be any that keep to these rules, and one draw needn't show every extreme that they name: `target_match_index`: each data group's row of positives is a permutation of 0 to 1023.
All inputs are finite; a program needn't handle non-finite values.
Results may differ from a plain program's by a relative error of at most 0.015.
Values may be sent and summed in bfloat16 or wider, within the bound.
No kernel may reach another device: no remote copies, remote signals or barrier semaphores. Data moves between devices by JAX's collectives and lax.ppermute only.
A program may use at most 64 MiB of HBM per device.

v0:
```python
import jax
import jax.numpy as jnp
from jax import lax
from jax.sharding import PartitionSpec as P

epsilon = 1e-06


def body(
    picture_vector_list,
    caption_latent_matrix,
    linear_map_matrix,
    target_match_index,
    sharpness_factor,
    offset_term,
):
    image_rows = picture_vector_list[0]
    hidden_rows = caption_latent_matrix[0]
    label_rows = target_match_index[0]
    row_count = image_rows.shape[0]
    blocks = lax.axis_size("blk")
    my_index = lax.axis_index("blk")
    multiplier_amount = sharpness_factor[0]
    offset_value = offset_term[0]
    piece_rows = linear_map_matrix.shape[0] // blocks
    w_piece = lax.dynamic_slice_in_dim(linear_map_matrix, my_index * piece_rows, piece_rows, 0)
    w_full = lax.all_gather(w_piece, ("group", "blk"), axis=0, tiled=True)
    hidden_chunk = lax.all_to_all(hidden_rows, "blk", split_axis=1, concat_axis=0, tiled=True)
    image_float = image_rows.astype(jnp.float32)
    image_scale = lax.rsqrt(jnp.sum(image_float * image_float, axis=1, keepdims=True) + epsilon)
    image_dir = image_float * image_scale
    image_unit = image_dir.astype(jnp.bfloat16)
    projected = jnp.dot(hidden_rows, w_full, preferred_element_type=jnp.float32)
    text_scale = lax.rsqrt(jnp.sum(projected * projected, axis=1, keepdims=True) + epsilon)
    text_dir = projected * text_scale
    text_unit = text_dir.astype(jnp.bfloat16)
    both = lax.all_gather(jnp.stack([image_unit, text_unit]), "blk", axis=1, tiled=True)
    image_all = both[0]
    text_all = both[1]
    label_all = lax.all_gather(label_rows.astype(jnp.float32), "blk", axis=0, tiled=True)

    def weights_of(logits, pair_sign):
        return (-pair_sign * jax.nn.sigmoid(-pair_sign * logits) * multiplier_amount).astype(
            jnp.bfloat16
        )

    scores = lax.dot_general(
        image_unit, text_all, (((1,), (1,)), ((), ())), preferred_element_type=jnp.float32
    )
    logits = multiplier_amount * scores + offset_value
    text_columns = jnp.arange(text_all.shape[0], dtype=jnp.int32)
    pair_sign = jnp.where(label_rows[:, None] == text_columns[None, :], 1.0, -1.0).astype(
        jnp.float32
    )
    loss_local = -jnp.sum(jax.nn.log_sigmoid(pair_sign * logits), axis=1)
    image_unit_grad = jnp.dot(
        weights_of(logits, pair_sign), text_all, preferred_element_type=jnp.float32
    )
    scores_t = lax.dot_general(
        image_all, text_unit, (((1,), (1,)), ((), ())), preferred_element_type=jnp.float32
    )
    logits_t = multiplier_amount * scores_t + offset_value
    own_columns = (my_index * row_count + jnp.arange(row_count, dtype=jnp.int32)).astype(
        jnp.float32
    )
    pair_sign_t = jnp.where(label_all[:, None] == own_columns[None, :], 1.0, -1.0).astype(
        jnp.float32
    )
    text_unit_grad = lax.dot_general(
        weights_of(logits_t, pair_sign_t),
        image_all,
        (((0,), (0,)), ((), ())),
        preferred_element_type=jnp.float32,
    )
    image_grad = (
        image_scale
        * (
            image_unit_grad
            - image_dir * jnp.sum(image_dir * image_unit_grad, axis=1, keepdims=True)
        )
    ).astype(jnp.bfloat16)
    projection_output_gradient = (
        text_scale
        * (text_unit_grad - text_dir * jnp.sum(text_dir * text_unit_grad, axis=1, keepdims=True))
    ).astype(jnp.bfloat16)
    grad_all = lax.all_gather(projection_output_gradient, "blk", axis=0, tiled=True)
    partial = lax.dot_general(
        hidden_chunk, grad_all, (((0,), (0,)), ((), ())), preferred_element_type=jnp.float32
    )
    projection_grad = lax.psum_scatter(partial, "group", scatter_dimension=0, tiled=True)
    return (loss_local[None], image_grad[None], projection_grad)


def solution(mesh):
    return jax.shard_map(
        body,
        mesh=mesh,
        in_specs=(
            P("group", "blk", None),
            P("group", "blk", None),
            P("group", None),
            P("group", "blk"),
            P(),
            P(),
        ),
        out_specs=(P("group", "blk"), P("group", "blk", None), P(("blk", "group"), None)),
        check_vma=False,
    )
```

profile of v0, /device:TPU:0, one launch (start us, length us, event | category | flops | bytes accessed | tf_op | source)
XLA Modules:
  0.0 220.5 jit_solution(2753661675826970912)
XLA Ops:
  7.2 0.0 all-gather.5.cloned.1.call-start
  7.2 1.0 copy-done
  8.2 0.7 constant_dynamic-slice_fusion
  8.9 0.0 all-gather.7.cloned.1.call-start
  9.0 1.2 copy.32
  10.2 0.1 fusion.37
  10.3 0.8 fusion.38
  11.1 66.6 %all-gather.5.cloned.1.call-done = bf16[3072,768]{1,0:T(8,128)(2,1)} async-done(((bf16[96,768]{1,0:T(8,128)(2,1)}), bf16[3072,768]{1,0:T(8,128)(2,1)}) %all-gather.5.cloned.1.call-update) | async-done | bytes 4718608 | tf_op jit(solution)/shard_map/all_gather | solution.py:27
  77.8 3.8 %multiply_reduce_fusion = (f32[256]{0:T(256)S(1)}, f32[768,256]{1,0:T(8,128)S(1)}) fusion(bf16[3072,768]{1,0:T(8,128)(2,1)} %all-gather.5.cloned.1.call-done, bf16[1,256,3072]{2,1,0:T(8,128)(2,1)S(1)} %copy-done.1), kind=kOutput, calls=%fused_computation.57 | convolution fusion | flops 1208352512 | bytes 7078912 | tf_op jit(solution)/shard_map/dot_general | solution.py:33
  81.6 0.1 fusion.55
  81.7 0.9 pad_maximum_fusion
  82.7 0.0 all-gather.7.cloned.1.call-update
  82.7 0.0 all-gather.9.cloned.1.call-start
  84.1 8.0 %all-gather = f32[4,1,256]{2,1,0:T(1,128)S(1)} all-gather(f32[1,1,256]{2,1,0:T(1,128)S(1)} %bitcast.120), channel_id=1, replica_groups=mesh['blk'=4,'group'=8] {'blk'}, dimensions={0}, use_global_device_ids=true | all-gather | bytes 5120 | tf_op jit(solution)/shard_map/all_gather | solution.py:40
  92.1 33.4 %all-gather.7.cloned.1.call-done = bf16[2,1024,768]{1,2,0:T(8,128)(2,1)} async-done(((bf16[2,256,768]{1,2,0:T(8,128)(2,1)}), bf16[2,1024,768]{1,2,0:T(8,128)(2,1)}) %all-gather.7.cloned.1.call-update) | async-done | bytes 3145744 | tf_op jit(solution)/shard_map/all_gather | solution.py:37
  125.5 4.6 %fusion.39 = (f32[256]{0:T(256)S(1)}, f32[256,768]{0,1:T(8,128)}) fusion(f32[768,256]{1,0:T(8,128)S(1)} %get-tuple-element.16, f32[256]{0:T(256)S(1)} %add_rsqrt_fusion, bf16[2,1024,768]{1,2,0:T(8,128)(2,1)} %all-gather.7.cloned.1.call-done, f32[]{:T(128)} %bitcast.115, f32[]{:T(128)} %bitcast.112, f32[256]{0:T(256)S(1)} %add_convert_fusion, ...), kind=kOutput, calls=%fused_computation.53 | convolution fusion | flops 809434880 | bytes 5513224 | tf_op jit(solution)/shard_map/dot_general | solution.py:69
  130.1 2.0 fusion.42
  132.1 0.0 all-gather.9.cloned.1.call-update
  132.2 0.0 reduce-scatter.4.cloned.1.call-start
  132.2 1.6 copy.37
  133.8 27.8 %all_to_all.19 = bf16[256,4,768]{0,2,1:T(8,128)(2,1)S(1)} all-to-all(bf16[256,4,768]{0,2,1:T(8,128)(2,1)} %bitcast.117), channel_id=1, replica_groups=mesh['blk'=4,'group'=8] {'blk'}, dimensions={1} | all-to-all | bytes 3145728 | tf_op jit(solution)/shard_map/all_to_all | solution.py:28
  161.6 1.6 copy.38
  163.2 9.1 %all-gather.9.cloned.1.call-done = bf16[1024,768]{0,1:T(8,128)(2,1)} async-done(((bf16[256,768]{0,1:T(8,128)(2,1)}), bf16[1024,768]{0,1:T(8,128)(2,1)}) %all-gather.9.cloned.1.call-update) | async-done | bytes 1572880 | tf_op jit(solution)/shard_map/all_gather | solution.py:86
  172.3 3.3 %convolution_bitcast_fusion = f32[768,768]{0,1:T(8,128)S(1)} fusion(bf16[1024,768]{0,1:T(8,128)(2,1)} %all-gather.9.cloned.1.call-done, bf16[1024,768]{1,0:T(8,128)(2,1)} %bitcast.118), kind=kOutput, calls=%fused_computation.1 | convolution fusion | flops 1207959552 | bytes 5505024 | tf_op jit(solution)/shard_map/dot_general | solution.py:87
  175.5 2.0 copy.43
  177.5 0.0 reduce-scatter.4.cloned.1.call-update
  177.6 1.0 copy-done.3
  178.5 3.5 %fusion.25 = (f32[256]{0:T(256)}, f32[256,1024]{1,0:T(8,128)S(1)}) fusion(s32[256]{0:T(256)S(1)} %bitcast.122, f32[]{:T(128)} %bitcast.114, bf16[2,1024,768]{1,2,0:T(8,128)(2,1)} %all-gather.7.cloned.1.call-done, bf16[1,256,768]{1,2,0:T(8,128)(2,1)S(1)} %copy-done.3, f32[]{:T(128)} %bitcast.111), kind=kOutput, calls=%fused_computation.31 | convolution fusion | flops 406060800 | bytes 3017728 | tf_op jit(solution)/shard_map/dot_general | solution.py:47
  182.0 1.0 fusion.33
  182.9 0.2 fusion.53
  183.1 0.9 copy.39
  184.0 29.9 %reduce-scatter.4.cloned.1.call-done = f32[96,768]{1,0:T(8,128)} async-done(((f32[768,768]{1,0:T(8,128)}), f32[96,768]{1,0:T(8,128)}) %reduce-scatter.4.cloned.1.call-update) | async-done | bytes 294928
  (15 shorter events, 0.1 us)
Async XLA Ops:
  7.2 1.1 copy-start
  7.2 70.6 %copy-start.1 = (bf16[1,256,3072]{2,1,0:T(8,128)(2,1)S(1)}, bf16[1,256,3072]{2,1,0:T(8,128)(2,1)}, u32[]{:S(2)}) copy-start(bf16[1,256,3072]{2,1,0:T(8,128)(2,1)} %param.7) | copy-start | bytes 4718596
  7.2 70.6 %all-gather.5.cloned.1.call-start = ((), (), s32[]{:S(2)}) async-start(), calls=%async_computation.2 | async-start | bytes 4866048 | tf_op jit(solution)/shard_map/all_gather | solution.py:27
  8.9 116.6 %all-gather.7.cloned.1.call-start = ((), (), s32[]{:S(2)}) async-start(), calls=%async_computation.3 | async-start | bytes 3932160 | tf_op jit(solution)/shard_map/all_gather | solution.py:37
  77.8 3.9 %copy-start.2 = (bf16[1,256,768]{1,2,0:T(8,128)(2,1)S(1)}, bf16[1,256,768]{1,2,0:T(8,128)(2,1)}, u32[]{:S(2)}) copy-start(bf16[1,256,768]{1,2,0:T(8,128)(2,1)} %fusion.38) | copy-start | bytes 1179652
  81.6 2.4 %copy-start.4 = (s32[1,256]{1,0:T(1,128)S(1)}, s32[1,256]{1,0:T(1,128)}, u32[]{:S(2)}) copy-start(s32[1,256]{1,0:T(1,128)} %param.9) | copy-start | bytes 3076
  82.7 89.6 %all-gather.9.cloned.1.call-start = ((), (), s32[]{:S(2)}) async-start(), calls=%async_computation.4 | async-start | bytes 1966080 | tf_op jit(solution)/shard_map/all_gather | solution.py:86
  132.2 81.8 %reduce-scatter.4.cloned.1.call-start = ((), (), s32[]{:S(2)}) async-start(), calls=%async_computation.5 | async-start | bytes 2654208
  177.5 1.0 copy-start.3
  178.5 3.5 %copy-start.5 = (bf16[2,1024,768]{1,2,0:T(8,128)(2,1)S(1)}, bf16[2,1024,768]{1,2,0:T(8,128)(2,1)}, u32[]{:S(2)}) copy-start(bf16[2,1024,768]{1,2,0:T(8,128)(2,1)} %all-gather.7.cloned.1.call-done) | copy-start | bytes 9437188
Sparse Core Ops, SparseCore 0:
  11.5 66.2 all-gather.4
  82.8 42.6 all-gather.6
  132.3 39.9 all-gather.8
  177.7 36.2 reduce-scatter.3
where the time goes:
time: 221 us; the launch traced here: 220 us
  waiting for transfers between devices  139 us (63%)
  blocking collectives  35.8 us (16%)
  matrix products  16.1 us (7%)
  between operations  15.2 us (7%)
  local copies, waits for them, and re-layouts  9.92 us (4%)
  other arithmetic  4.17 us (2%)
    all_gather x1, waiting for transfers between devices, body(): w_full = lax.all_gather(w_piece, ('group', 'blk'), axis=0, tiled=True)  66.6 us
    all_gather x1, waiting for transfers between devices, body(): lax.all_gather(jnp.stack([image_unit, text_unit]), 'blk', axis=1, tiled=T...  33.4 us
    unnamed x5, waiting for transfers between devices  30 us
    all_to_all x1, blocking collectives, body(): lax.all_to_all(hidden_rows, 'blk', split_axis=1, concat_axis=0, tiled=True)  27.8 us
    all_gather x1, waiting for transfers between devices, body(): lax.all_gather(projection_output_gradient, 'blk', axis=0, tiled=True)  9.09 us
    all_gather x1, blocking collectives, body(): lax.all_gather(label_rows.astype(jnp.float32), 'blk', axis=0, tiled=True)  8.03 us
    unnamed x16, local copies, waits for them, and re-layouts  7.66 us
    dot_general x1, matrix products, body(): lax.dot_general(weights_of(logits_t, pair_sign_t), image_all, (((0,), (0,...  4.64 us
  transfers between devices with their start and end apart: 4, of which 4 were waited for; matrix products, arithmetic and copies ran while one was open for 5% of the time, Pallas kernels for 0%

commit v1 on v0

--- a/solution.py
+++ b/solution.py
@@ -25,7 +25,12 @@
     piece_rows = linear_map_matrix.shape[0] // blocks
     w_piece = lax.dynamic_slice_in_dim(linear_map_matrix, my_index * piece_rows, piece_rows, 0)
     w_full = lax.all_gather(w_piece, ("group", "blk"), axis=0, tiled=True)
-    hidden_chunk = lax.all_to_all(hidden_rows, "blk", split_axis=1, concat_axis=0, tiled=True)
+    hidden_chunk = jnp.concatenate(
+        lax.all_to_all(
+            jnp.stack(jnp.split(hidden_rows, lax.axis_size("blk"), axis=1)), "blk", 0, 0
+        ),
+        axis=0,
+    )
     image_float = image_rows.astype(jnp.float32)
     image_scale = lax.rsqrt(jnp.sum(image_float * image_float, axis=1, keepdims=True) + epsilon)
     image_dir = image_float * image_scale

time: 221 us -> 220 us (level)
  local copies, waits for them, and re-layouts: 9.92 us -> 4.85 us
  waiting for transfers between devices: 139 us -> 143 us
    unnamed x5 -> x4, waiting for transfers between devices: 30 us -> 0.07 us
    reduce_scatter x0 -> x1, waiting for transfers between devices: none -> 29.9 us  [body(): lax.psum_scatter(partial, 'group', scatter_dimension=0, tiled=True)]
    all_gather x1, waiting for transfers between devices: 9.09 us -> 13 us  [body(): lax.all_gather(projection_output_gradient, 'blk', axis=0, tiled=True)]
    unnamed x16 -> x14, local copies, waits for them, and re-layouts: 7.66 us -> 4.08 us
  transfers between devices with their start and end apart: 4 -> 4, of which waited for: 4 -> 4; matrix products, arithmetic and copies ran while one was open for 5% -> 4% of each run, Pallas kernels for 0% -> 0%
where the time goes in v1:
time: 220 us
  waiting for transfers between devices  143 us (65%)
  blocking collectives  34.7 us (16%)
  matrix products  17.3 us (8%)
  between operations  15.2 us (7%)
  local copies, waits for them, and re-layouts  4.85 us (2%)
  other arithmetic  4.38 us (2%)
    all_gather x1, waiting for transfers between devices, body(): w_full = lax.all_gather(w_piece, ('group', 'blk'), axis=0, tiled=True)  66.6 us
    all_gather x1, waiting for transfers between devices, body(): lax.all_gather(jnp.stack([image_unit, text_unit]), 'blk', axis=1, tiled=T...  33.4 us
    reduce_scatter x1, waiting for transfers between devices, body(): lax.psum_scatter(partial, 'group', scatter_dimension=0, tiled=True)  29.9 us
    all_to_all x1, blocking collectives, body(): lax.all_to_all(jnp.stack(jnp.split(hidden_rows, lax.axis_size('blk'), axi...  26.7 us
    all_gather x1, waiting for transfers between devices, body(): lax.all_gather(projection_output_gradient, 'blk', axis=0, tiled=True)  13 us
    all_gather x1, blocking collectives, body(): lax.all_gather(label_rows.astype(jnp.float32), 'blk', axis=0, tiled=True)  8.03 us
    dot_general x1, matrix products, body(): lax.dot_general(weights_of(logits_t, pair_sign_t), image_all, (((0,), (0,...  4.7 us
  transfers between devices with their start and end apart: 4, of which 4 were waited for; matrix products, arithmetic and copies ran while one was open for 4% of the time, Pallas kernels for 0%

profile of v1, /device:TPU:0, one launch (start us, length us, event | category | flops | bytes accessed | tf_op | source)
XLA Modules:
  0.0 219.6 jit_solution(5348522946042424322)
XLA Ops:
  7.2 0.0 all-gather.5.cloned.1.call-start
  7.2 1.0 copy-done
  8.2 0.7 constant_dynamic-slice_fusion
  8.9 0.0 all-gather.5.cloned.1.call-update
  8.9 0.0 all-gather.7.cloned.1.call-start
  9.0 1.2 copy.15
  10.2 0.1 fusion.35
  10.3 0.8 fusion.36
  11.1 66.6 %all-gather.5.cloned.1.call-done = bf16[3072,768]{1,0:T(8,128)(2,1)} async-done(((bf16[96,768]{1,0:T(8,128)(2,1)}), bf16[3072,768]{1,0:T(8,128)(2,1)}) %all-gather.5.cloned.1.call-update) | async-done | bytes 4718608 | tf_op jit(solution)/shard_map/all_gather | solution.py:27
  77.8 3.8 %multiply_reduce_fusion = (f32[256]{0:T(256)S(1)}, f32[768,256]{1,0:T(8,128)S(1)}) fusion(bf16[3072,768]{1,0:T(8,128)(2,1)} %all-gather.5.cloned.1.call-done, bf16[1,256,3072]{2,1,0:T(8,128)(2,1)S(1)} %copy-done.1), kind=kOutput, calls=%fused_computation.55 | convolution fusion | flops 1208352512 | bytes 7078912 | tf_op jit(solution)/shard_map/dot_general | solution.py:38
  81.6 0.1 fusion.53
  81.7 0.9 pad_maximum_fusion.1
  82.7 0.0 all-gather.7.cloned.1.call-update
  82.7 0.0 all-gather.9.cloned.1.call-start
  84.1 8.0 %all-gather = f32[4,1,256]{2,1,0:T(1,128)S(1)} all-gather(f32[1,1,256]{2,1,0:T(1,128)S(1)} %bitcast.122), channel_id=1, replica_groups=mesh['blk'=4,'group'=8] {'blk'}, dimensions={0}, use_global_device_ids=true | all-gather | bytes 5120 | tf_op jit(solution)/shard_map/all_gather | solution.py:45
  92.1 33.4 %all-gather.7.cloned.1.call-done = bf16[2,1024,768]{1,2,0:T(8,128)(2,1)} async-done(((bf16[2,256,768]{1,2,0:T(8,128)(2,1)}), bf16[2,1024,768]{1,2,0:T(8,128)(2,1)}) %all-gather.7.cloned.1.call-update) | async-done | bytes 3145744 | tf_op jit(solution)/shard_map/all_gather | solution.py:42
  125.5 4.7 %fusion.37 = (f32[256]{0:T(256)S(1)}, f32[256,768]{0,1:T(8,128)}) fusion(f32[768,256]{1,0:T(8,128)S(1)} %get-tuple-element.14, f32[256]{0:T(256)S(1)} %add_rsqrt_fusion, bf16[2,1024,768]{1,2,0:T(8,128)(2,1)} %all-gather.7.cloned.1.call-done, f32[]{:T(128)} %bitcast.118, f32[]{:T(128)} %bitcast.115, f32[256]{0:T(256)S(1)} %add_convert_fusion, ...), kind=kOutput, calls=%fused_computation.51 | convolution fusion | flops 809434880 | bytes 5513224 | tf_op jit(solution)/shard_map/dot_general | solution.py:74
  130.2 2.0 fusion.40
  132.2 0.0 all-gather.9.cloned.1.call-update
  132.2 0.0 reduce-scatter.2.cloned.1.call-start
  132.3 0.1 slice_bitcast_fusion.35
  132.4 0.2 pad_maximum_fusion
  132.6 26.7 %all_to_all.5 = bf16[4,256,768]{2,1,0:T(8,128)(2,1)S(1)} all-to-all(bf16[4,256,768]{2,1,0:T(8,128)(2,1)S(1)} %pad_maximum_fusion), channel_id=1, replica_groups=mesh['blk'=4,'group'=8] {'blk'}, dimensions={0} | all-to-all | bytes 3145728 | tf_op jit(solution)/shard_map/all_to_all | solution.py:29
  159.3 13.0 %all-gather.9.cloned.1.call-done = bf16[1024,768]{0,1:T(8,128)(2,1)} async-done(((bf16[256,768]{0,1:T(8,128)(2,1)}), bf16[1024,768]{0,1:T(8,128)(2,1)}) %all-gather.9.cloned.1.call-update) | async-done | bytes 1572880 | tf_op jit(solution)/shard_map/all_gather | solution.py:91
  172.3 4.3 %fusion.60 = f32[768,768]{1,0:T(8,128)} fusion(bf16[1024,768]{1,0:T(8,128)(2,1)S(1)} %bitcast.120, bf16[1024,768]{0,1:T(8,128)(2,1)} %all-gather.9.cloned.1.call-done), kind=kOutput, calls=%fused_computation.83 | convolution fusion | flops 1207959552 | bytes 5505024 | tf_op jit(solution)/shard_map/dot_general | solution.py:92
  176.6 0.0 reduce-scatter.2.cloned.1.call-update
  176.7 1.0 copy-done.3
  177.6 3.5 %fusion.23 = (f32[256]{0:T(256)}, f32[256,1024]{1,0:T(8,128)S(1)}) fusion(s32[256]{0:T(256)S(1)} %bitcast.124, f32[]{:T(128)} %bitcast.117, bf16[2,1024,768]{1,2,0:T(8,128)(2,1)} %all-gather.7.cloned.1.call-done, bf16[1,256,768]{1,2,0:T(8,128)(2,1)S(1)} %copy-done.3, f32[]{:T(128)} %bitcast.114), kind=kOutput, calls=%fused_computation.29 | convolution fusion | flops 406060800 | bytes 3017728 | tf_op jit(solution)/shard_map/dot_general | solution.py:52
  181.1 1.0 fusion.31
  182.1 0.1 fusion.51
  182.2 0.9 copy.20
  183.1 29.9 %reduce-scatter.2.cloned.1.call-done = f32[96,768]{1,0:T(8,128)} async-done(((f32[768,768]{1,0:T(8,128)}), f32[96,768]{1,0:T(8,128)}) %reduce-scatter.2.cloned.1.call-update) | async-done | bytes 294928 | tf_op jit(solution)/shard_map/reduce_scatter | solution.py:95
  (14 shorter events, 0.0 us)
Async XLA Ops:
  7.2 1.1 copy-start
  7.2 70.6 %copy-start.1 = (bf16[1,256,3072]{2,1,0:T(8,128)(2,1)S(1)}, bf16[1,256,3072]{2,1,0:T(8,128)(2,1)}, u32[]{:S(2)}) copy-start(bf16[1,256,3072]{2,1,0:T(8,128)(2,1)} %param.7) | copy-start | bytes 4718596
  7.2 70.6 %all-gather.5.cloned.1.call-start = ((), (), s32[]{:S(2)}) async-start(), calls=%async_computation.2 | async-start | bytes 4866048 | tf_op jit(solution)/shard_map/all_gather | solution.py:27
  8.9 116.6 %all-gather.7.cloned.1.call-start = ((), (), s32[]{:S(2)}) async-start(), calls=%async_computation.3 | async-start | bytes 3932160 | tf_op jit(solution)/shard_map/all_gather | solution.py:42
  77.8 4.0 %copy-start.2 = (bf16[1,256,768]{1,2,0:T(8,128)(2,1)S(1)}, bf16[1,256,768]{1,2,0:T(8,128)(2,1)}, u32[]{:S(2)}) copy-start(bf16[1,256,768]{1,2,0:T(8,128)(2,1)} %fusion.36) | copy-start | bytes 1179652
  81.6 2.4 %copy-start.4 = (s32[1,256]{1,0:T(1,128)S(1)}, s32[1,256]{1,0:T(1,128)}, u32[]{:S(2)}) copy-start(s32[1,256]{1,0:T(1,128)} %param.9) | copy-start | bytes 3076
  82.7 89.7 %all-gather.9.cloned.1.call-start = ((), (), s32[]{:S(2)}) async-start(), calls=%async_computation.4 | async-start | bytes 1966080 | tf_op jit(solution)/shard_map/all_gather | solution.py:91
  132.2 80.8 %reduce-scatter.2.cloned.1.call-start = ((), (), s32[]{:S(2)}) async-start(), calls=%async_computation.5 | async-start | bytes 2654208 | tf_op jit(solution)/shard_map/reduce_scatter | solution.py:95
  176.6 1.0 copy-start.3
  177.6 3.5 %copy-start.5 = (bf16[2,1024,768]{1,2,0:T(8,128)(2,1)S(1)}, bf16[2,1024,768]{1,2,0:T(8,128)(2,1)}, u32[]{:S(2)}) copy-start(bf16[2,1024,768]{1,2,0:T(8,128)(2,1)} %all-gather.7.cloned.1.call-done) | copy-start | bytes 9437188
Sparse Core Ops, SparseCore 0:
  11.5 66.2 all-gather.4
  82.8 42.6 all-gather.6
  132.4 39.9 all-gather.8
  176.8 36.2 reduce-scatter.1
